TPU v7x, 256 devices: a whole 4x4x8 slice. The times are simulated.
256 devices in a mesh: dp: 16 (over y, x), section: 2 (over core), tensor: 8 (over z).
Axes of the slice: x: 4, y: 4, z: 8, core: 2. Of those that a mesh axis runs over, the one named last changes fastest.
Arguments:
- tokens: bfloat16 [2048, 16384], P('dp'), may hold values from -9 to 9
- order: int32 [2048], replicated, may hold values from 0 to 2047, as said below
- segments: int32 [2048], replicated, may hold values from 0 to 1, as said below
- gain: float32 [2, 16384], P('section', 'dp'), may hold values from 0.1 to 1.9
- w_query: bfloat16 [2, 16384, 8192], P('section', 'dp', 'tensor'), may hold values from -0.046875 to 0.046875
- key_value_weight: bfloat16 [2, 16384, 8, 256], P('section', 'dp', 'tensor'), may hold values from -0.046875 to 0.046875
- w_out: bfloat16 [2, 8192, 16384], P('section', 'tensor', 'dp'), may hold values from -0.0625 to 0.0625
Outputs:
- layer_out: bfloat16 [2048, 16384], P('section', 'dp')
Inputs may be any that keep to these rules, and one draw needn't show every extreme that they name: A permutation that moves whole sentences: the rows of one sentence (a run of equal segments within a block of 32 rows) come from consecutive entry rows in order. `segments`: within each block of 32 rows the sentence numbers do not fall and each of 0 to 1 appears.
All inputs are finite; a program needn't handle non-finite values.
Results may differ from a plain program's by a relative error of at most 0.022.
Values may be sent and summed in bfloat16 or wider, within the bound.
No kernel may reach another device: no remote copies, remote signals or barrier semaphores. Data moves between devices by JAX's collectives and lax.ppermute only.
A program may use at most 64 MiB of HBM per device.

v0:
```python
import math
import jax
import jax.numpy as jnp
from jax import lax
from jax.sharding import PartitionSpec as P

MODEL_WIDTH = 16384
KEYVALUE_HEADS = 8
QUERY_HEADS = 64
MICRO_TOKENS = 32
M = 4
norm_epsilon = 1e-05


def passed_along(array, axis, by):
    count = lax.axis_size(axis)
    return lax.ppermute(array, axis, [(i, (i + by) % count) for i in range(count)])


def causal_block_attend(query_rows, key_value_rows, sentence_segment_rows, query_group_width):
    row_count = query_rows.shape[0]
    kv_heads = key_value_rows.shape[1]
    head_size = key_value_rows.shape[2] // 2
    query_head_rows = query_rows.reshape(row_count, kv_heads, query_group_width, head_size)
    key_heads = key_value_rows[:, :, :head_size]
    value_heads = key_value_rows[:, :, head_size:]
    scores = jnp.einsum(
        "qkgd,skd->kgqs", query_head_rows, key_heads, preferred_element_type=jnp.float32
    ) / math.sqrt(head_size)
    position = jnp.arange(row_count)
    allowed = (sentence_segment_rows[:, None] == sentence_segment_rows[None, :]) & (
        position[None, :] <= position[:, None]
    )
    raw_weights = jnp.where(allowed[None, None], jnp.exp(scores), 0.0)
    totals = jnp.sum(raw_weights, axis=-1, keepdims=True)
    probs = (raw_weights / totals).astype(jnp.bfloat16)
    attended_rows = jnp.einsum(
        "kgqs,skd->qkgd", probs, value_heads, preferred_element_type=jnp.float32
    )
    return attended_rows.astype(jnp.bfloat16).reshape(
        row_count, kv_heads * query_group_width * head_size
    )


def section_layer(
    hidden, sentence_segment_rows, gain_row, query_weight, key_value_matrix, out_weight
):
    slice_width = hidden.shape[1]
    own_rows = sentence_segment_rows.shape[0]
    own_start = lax.axis_index("dp") * own_rows
    widened = hidden.astype(jnp.float32)
    normed_rows = (widened * gain_row[None, :]).astype(jnp.bfloat16)
    query_terms = jnp.dot(normed_rows, query_weight, preferred_element_type=jnp.float32)
    keyval_terms = jnp.dot(
        normed_rows, key_value_matrix.reshape(slice_width, -1), preferred_element_type=jnp.float32
    )
    square_terms = jnp.sum(widened * widened, axis=1)
    all_squares = lax.psum(square_terms, "dp")
    own_squares = lax.dynamic_slice_in_dim(all_squares, own_start, own_rows)
    query_sums, keyval_sums = (
        lax.psum_scatter(
            query_terms.astype(jnp.bfloat16), "dp", scatter_dimension=0, tiled=True
        ).astype(jnp.float32),
        lax.psum_scatter(
            keyval_terms.astype(jnp.bfloat16), "dp", scatter_dimension=0, tiled=True
        ).astype(jnp.float32),
    )
    root_mean_square = jnp.sqrt(own_squares / MODEL_WIDTH + norm_epsilon)
    query_rows = (query_sums / root_mean_square[:, None]).astype(jnp.bfloat16)
    kv_heads = key_value_matrix.shape[1]
    key_value_rows = (
        (keyval_sums / root_mean_square[:, None])
        .astype(jnp.bfloat16)
        .reshape(own_rows, kv_heads, key_value_matrix.shape[2])
    )
    attended_rows = causal_block_attend(
        query_rows, key_value_rows, sentence_segment_rows, QUERY_HEADS // KEYVALUE_HEADS
    )
    head_terms = jnp.dot(
        lax.all_gather(attended_rows, "dp", axis=0, tiled=True),
        out_weight,
        preferred_element_type=jnp.float32,
    )
    head_total = lax.psum(head_terms.astype(jnp.bfloat16), "tensor").astype(jnp.float32)
    return (widened + head_total).astype(jnp.bfloat16)


def on_device(tokens, order, segments, gain, w_query, key_value_weight, w_out):
    spread = lax.all_to_all(tokens, "dp", split_axis=1, concat_axis=0, tiled=True)
    arranged = jnp.take(spread, order, axis=0)
    group_count = lax.axis_size("dp")
    rows_all = group_count * MICRO_TOKENS
    section_index = lax.axis_index("section")
    group_index = lax.axis_index("dp")
    gain_row = gain[0]
    query_weight = w_query[0]
    key_value_matrix = key_value_weight[0]
    out_weight = w_out[0]
    received = jnp.zeros((rows_all, arranged.shape[1]), jnp.bfloat16)
    inbox = []
    results = []
    for turn_index in range(M + 1):
        if turn_index < M:
            fresh = arranged[turn_index * rows_all : (turn_index + 1) * rows_all]
        else:
            fresh = jnp.zeros_like(received)
        micro_index = jnp.where(
            section_index == 0, min(turn_index, M - 1), max(turn_index - 1, 0)
        ).astype(jnp.int32)
        sentence_segment_rows = lax.dynamic_slice_in_dim(
            segments, micro_index * rows_all + group_index * MICRO_TOKENS, MICRO_TOKENS
        )
        layer_input = jnp.where(section_index == 0, fresh, received)
        layer_output = section_layer(
            layer_input, sentence_segment_rows, gain_row, query_weight, key_value_matrix, out_weight
        )
        inbox.append(received)
        results.append(layer_output)
        if turn_index < M:
            received = passed_along(layer_output, "section", 1)
    half_count = M // 2
    from_back = jnp.concatenate(
        [inbox[index_value + 2] for index_value in range(half_count)], axis=0
    )
    kept_here = jnp.concatenate(
        [results[index_value + 1] for index_value in range(half_count, M)], axis=0
    )
    return jnp.where(section_index == 0, from_back, kept_here)


def solution(mesh):
    placed = (
        P("dp", None),
        P(),
        P(),
        P("section", "dp"),
        P("section", "dp", "tensor"),
        P("section", "dp", "tensor", None),
        P("section", "tensor", "dp"),
    )
    return jax.shard_map(
        on_device, mesh=mesh, in_specs=placed, out_specs=P("section", "dp"), check_vma=False
    )
```

profile of v0, /device:TPU:2, one launch (start us, length us, event | category | flops | bytes accessed | tf_op | source)
XLA Modules:
  0.0 1587.2 jit_solution(1069376487911914419)
XLA Ops:
  6.5 4.9 copy.87
  11.5 7.6 all-to-all-start
  19.2 59.1 %all-to-all-done = bf16[128,16,1024]{2,0,1:T(8,128)(2,1)} async-done(((bf16[128,16,1024]{2,0,1:T(8,128)(2,1)}), bf16[128,16,1024]{2,0,1:T(8,128)(2,1)}, u32[]{:S(2)}, u32[]{:S(2)}) %all-to-all-start) | async-done | bytes 4194336 | tf_op jit(solution)/shard_map/all_to_all | solution.py:89
  78.3 13.7 gather_fusion
  103.8 39.7 %psum.70 = f32[512]{0:T(512)S(1)} all-reduce(f32[512]{0:T(512)S(1)} %fusion.1), channel_id=1, replica_groups=mesh['dp'=16,'section'=2,'tensor'=8] {'dp'}, use_global_device_ids=true, to_apply=%region_2.3 | all-reduce | flops 512 | bytes 4096 | tf_op jit(solution)/shard_map/psum | solution.py:58
  143.6 36.6 %reduce-scatter.11.cloned.1.call-done = bf16[32,256]{1,0:T(8,128)(2,1)} async-done(((bf16[512,256]{1,0:T(8,128)(2,1)}), bf16[32,256]{1,0:T(8,128)(2,1)}) %reduce-scatter.11.cloned.1.call-update) | async-done | bytes 16400 | tf_op jit(solution)/shard_map/reduce_scatter | solution.py:64
  181.0 81.3 %reduce-scatter.13.cloned.1.call-done = bf16[32,1024]{1,0:T(8,128)(2,1)} async-done(((bf16[512,1024]{1,0:T(8,128)(2,1)}), bf16[32,1024]{1,0:T(8,128)(2,1)}) %reduce-scatter.13.cloned.1.call-update) | async-done | bytes 65552 | tf_op jit(solution)/shard_map/reduce_scatter | solution.py:61
  264.4 47.2 %all-gather.6.cloned.1.call-done = bf16[512,1024]{1,0:T(8,128)(2,1)} async-done(((bf16[32,1024]{1,0:T(8,128)(2,1)}), bf16[512,1024]{1,0:T(8,128)(2,1)}) %all-gather.6.cloned.1.call-update) | async-done | bytes 1048592 | tf_op jit(solution)/shard_map/all_gather | solution.py:80
  315.8 75.8 %all-reduce.6.cloned.1.call-done = bf16[512,1024]{1,0:T(8,128)(2,1)} async-done(((bf16[512,1024]{1,0:T(8,128)(2,1)}), bf16[512,1024]{1,0:T(8,128)(2,1)}) %all-reduce.6.cloned.1.call-update) | async-done | bytes 1048592 | tf_op jit(solution)/shard_map/psum | solution.py:84
  401.6 36.4 %psum.72 = f32[512]{0:T(512)S(1)} all-reduce(f32[512]{0:T(512)S(1)} %get-tuple-element.9), channel_id=1, replica_groups=mesh['dp'=16,'section'=2,'tensor'=8] {'dp'}, use_global_device_ids=true, to_apply=%region_8.9 | all-reduce | flops 512 | bytes 4096 | tf_op jit(solution)/shard_map/psum | solution.py:58
  438.1 37.8 %reduce-scatter.15.cloned.1.call-done = bf16[32,256]{1,0:T(8,128)(2,1)} async-done(((bf16[512,256]{1,0:T(8,128)(2,1)}), bf16[32,256]{1,0:T(8,128)(2,1)}) %reduce-scatter.15.cloned.1.call-update) | async-done | bytes 16400 | tf_op jit(solution)/shard_map/reduce_scatter | solution.py:64
  476.6 80.9 %reduce-scatter.17.cloned.1.call-done = bf16[32,1024]{1,0:T(8,128)(2,1)} async-done(((bf16[512,1024]{1,0:T(8,128)(2,1)}), bf16[32,1024]{1,0:T(8,128)(2,1)}) %reduce-scatter.17.cloned.1.call-update) | async-done | bytes 65552 | tf_op jit(solution)/shard_map/reduce_scatter | solution.py:61
  559.7 47.2 %all-gather.8.cloned.1.call-done = bf16[512,1024]{1,0:T(8,128)(2,1)} async-done(((bf16[32,1024]{1,0:T(8,128)(2,1)}), bf16[512,1024]{1,0:T(8,128)(2,1)}) %all-gather.8.cloned.1.call-update) | async-done | bytes 1048592 | tf_op jit(solution)/shard_map/all_gather | solution.py:80
  611.1 75.8 %all-reduce.8.cloned.1.call-done = bf16[512,1024]{1,0:T(8,128)(2,1)} async-done(((bf16[512,1024]{1,0:T(8,128)(2,1)}), bf16[512,1024]{1,0:T(8,128)(2,1)}) %all-reduce.8.cloned.1.call-update) | async-done | bytes 1048592 | tf_op jit(solution)/shard_map/psum | solution.py:84
  699.0 36.4 %psum.74 = f32[512]{0:T(512)S(1)} all-reduce(f32[512]{0:T(512)S(1)} %get-tuple-element.7), channel_id=1, replica_groups=mesh['dp'=16,'section'=2,'tensor'=8] {'dp'}, use_global_device_ids=true, to_apply=%region_14.15 | all-reduce | flops 512 | bytes 4096 | tf_op jit(solution)/shard_map/psum | solution.py:58
  735.5 36.5 %reduce-scatter.19.cloned.1.call-done = bf16[32,256]{1,0:T(8,128)(2,1)} async-done(((bf16[512,256]{1,0:T(8,128)(2,1)}), bf16[32,256]{1,0:T(8,128)(2,1)}) %reduce-scatter.19.cloned.1.call-update) | async-done | bytes 16400 | tf_op jit(solution)/shard_map/reduce_scatter | solution.py:64
  772.7 81.0 %reduce-scatter.21.cloned.1.call-done = bf16[32,1024]{1,0:T(8,128)(2,1)} async-done(((bf16[512,1024]{1,0:T(8,128)(2,1)}), bf16[32,1024]{1,0:T(8,128)(2,1)}) %reduce-scatter.21.cloned.1.call-update) | async-done | bytes 65552 | tf_op jit(solution)/shard_map/reduce_scatter | solution.py:61
  855.9 47.2 %all-gather.10.cloned.1.call-done = bf16[512,1024]{1,0:T(8,128)(2,1)} async-done(((bf16[32,1024]{1,0:T(8,128)(2,1)}), bf16[512,1024]{1,0:T(8,128)(2,1)}) %all-gather.10.cloned.1.call-update) | async-done | bytes 1048592 | tf_op jit(solution)/shard_map/all_gather | solution.py:80
  903.1 4.2 fusion.56
  907.4 75.8 %all-reduce.10.cloned.1.call-done = bf16[512,1024]{1,0:T(8,128)(2,1)} async-done(((bf16[512,1024]{1,0:T(8,128)(2,1)}), bf16[512,1024]{1,0:T(8,128)(2,1)}) %all-reduce.10.cloned.1.call-update) | async-done | bytes 1048592 | tf_op jit(solution)/shard_map/psum | solution.py:84
  996.5 36.4 %psum.76 = f32[512]{0:T(512)S(1)} all-reduce(f32[512]{0:T(512)S(1)} %get-tuple-element.5), channel_id=1, replica_groups=mesh['dp'=16,'section'=2,'tensor'=8] {'dp'}, use_global_device_ids=true, to_apply=%region_20.21 | all-reduce | flops 512 | bytes 4096 | tf_op jit(solution)/shard_map/psum | solution.py:58
  1032.9 36.5 %reduce-scatter.23.cloned.1.call-done = bf16[32,256]{1,0:T(8,128)(2,1)} async-done(((bf16[512,256]{1,0:T(8,128)(2,1)}), bf16[32,256]{1,0:T(8,128)(2,1)}) %reduce-scatter.23.cloned.1.call-update) | async-done | bytes 16400 | tf_op jit(solution)/shard_map/reduce_scatter | solution.py:64
  1070.2 80.9 %reduce-scatter.25.cloned.1.call-done = bf16[32,1024]{1,0:T(8,128)(2,1)} async-done(((bf16[512,1024]{1,0:T(8,128)(2,1)}), bf16[32,1024]{1,0:T(8,128)(2,1)}) %reduce-scatter.25.cloned.1.call-update) | async-done | bytes 65552 | tf_op jit(solution)/shard_map/reduce_scatter | solution.py:61
  1153.2 47.1 %all-gather.12.cloned.1.call-done = bf16[512,1024]{1,0:T(8,128)(2,1)} async-done(((bf16[32,1024]{1,0:T(8,128)(2,1)}), bf16[512,1024]{1,0:T(8,128)(2,1)}) %all-gather.12.cloned.1.call-update) | async-done | bytes 1048592 | tf_op jit(solution)/shard_map/all_gather | solution.py:80
  1200.3 4.2 fusion.59
  1204.5 75.8 %all-reduce.12.cloned.1.call-done = bf16[512,1024]{1,0:T(8,128)(2,1)} async-done(((bf16[512,1024]{1,0:T(8,128)(2,1)}), bf16[512,1024]{1,0:T(8,128)(2,1)}) %all-reduce.12.cloned.1.call-update) | async-done | bytes 1048592 | tf_op jit(solution)/shard_map/psum | solution.py:84
  1291.0 36.4 %psum.78 = f32[512]{0:T(512)S(1)} all-reduce(f32[512]{0:T(512)S(1)} %fusion.13), channel_id=1, replica_groups=mesh['dp'=16,'section'=2,'tensor'=8] {'dp'}, use_global_device_ids=true, to_apply=%region_26.27 | all-reduce | flops 512 | bytes 4096 | tf_op jit(solution)/shard_map/psum | solution.py:58
  1327.5 37.4 %reduce-scatter.27.cloned.1.call-done = bf16[32,256]{1,0:T(8,128)(2,1)} async-done(((bf16[512,256]{1,0:T(8,128)(2,1)}), bf16[32,256]{1,0:T(8,128)(2,1)}) %reduce-scatter.27.cloned.1.call-update) | async-done | bytes 16400 | tf_op jit(solution)/shard_map/reduce_scatter | solution.py:64
  1365.7 81.0 %reduce-scatter.29.cloned.1.call-done = bf16[32,1024]{1,0:T(8,128)(2,1)} async-done(((bf16[512,1024]{1,0:T(8,128)(2,1)}), bf16[32,1024]{1,0:T(8,128)(2,1)}) %reduce-scatter.29.cloned.1.call-update) | async-done | bytes 65552 | tf_op jit(solution)/shard_map/reduce_scatter | solution.py:61
  1449.0 47.0 %all-gather.14.cloned.1.call-done = bf16[512,1024]{1,0:T(8,128)(2,1)} async-done(((bf16[32,1024]{1,0:T(8,128)(2,1)}), bf16[512,1024]{1,0:T(8,128)(2,1)}) %all-gather.14.cloned.1.call-update) | async-done | bytes 1048592 | tf_op jit(solution)/shard_map/all_gather | solution.py:80
  1496.0 4.2 fusion.62
  1500.2 75.9 %all-reduce.14.cloned.1.call-done = bf16[512,1024]{1,0:T(8,128)(2,1)} async-done(((bf16[512,1024]{1,0:T(8,128)(2,1)}), bf16[512,1024]{1,0:T(8,128)(2,1)}) %all-reduce.14.cloned.1.call-update) | async-done | bytes 1048592 | tf_op jit(solution)/shard_map/psum | solution.py:84
  (142 shorter events, 85.3 us)
Async XLA Ops:
  6.5 91.2 %copy-start = (bf16[1,1024,1024]{2,1,0:T(8,128)(2,1)S(1)}, bf16[1,1024,1024]{2,1,0:T(8,128)(2,1)}, u32[]{:S(2)}) copy-start(bf16[1,1024,1024]{2,1,0:T(8,128)(2,1)} %param.11) | copy-start | bytes 6291460
  11.5 7.7 copy-start.9
  11.5 66.8 %all-to-all-start = ((bf16[128,16,1024]{2,0,1:T(8,128)(2,1)}), bf16[128,16,1024]{2,0,1:T(8,128)(2,1)}, u32[]{:S(2)}, u32[]{:S(2)}) async-start(bf16[128,16,1024]{2,0,1:T(8,128)(2,1)} %bitcast.266), calls=%async_computation | async-start | bytes 8388608 | tf_op jit(solution)/shard_map/all_to_all | solution.py:89
  19.1 161.1 %reduce-scatter.11.cloned.1.call-start = ((), (), s32[]{:S(2)}) async-start(), calls=%async_computation.11 | async-start | bytes 278528 | tf_op jit(solution)/shard_map/reduce_scatter | solution.py:64
  92.0 4.5 copy-start.10
  92.0 4.5 copy-start.15
  97.7 164.5 %reduce-scatter.13.cloned.1.call-start = ((), (), s32[]{:S(2)}) async-start(), calls=%async_computation.12 | async-start | bytes 1114112 | tf_op jit(solution)/shard_map/reduce_scatter | solution.py:61
  101.2 210.3 %all-gather.6.cloned.1.call-start = ((), (), s32[]{:S(2)}) async-start(), calls=%async_computation.13 | async-start | bytes 1114112 | tf_op jit(solution)/shard_map/all_gather | solution.py:80
  264.3 127.3 %all-reduce.6.cloned.1.call-start = ((), (), s32[]{:S(2)}) async-start(), calls=%async_computation.14 | async-start | bytes 2097152 | tf_op jit(solution)/shard_map/psum | solution.py:84
  315.7 160.1 %reduce-scatter.15.cloned.1.call-start = ((), (), s32[]{:S(2)}) async-start(), calls=%async_computation.15 | async-start | bytes 278528 | tf_op jit(solution)/shard_map/reduce_scatter | solution.py:64
  393.6 2.7 collective-permute-start
  399.2 158.4 %reduce-scatter.17.cloned.1.call-start = ((), (), s32[]{:S(2)}) async-start(), calls=%async_computation.16 | async-start | bytes 1114112 | tf_op jit(solution)/shard_map/reduce_scatter | solution.py:61
  401.5 205.4 %all-gather.8.cloned.1.call-start = ((), (), s32[]{:S(2)}) async-start(), calls=%async_computation.17 | async-start | bytes 1114112 | tf_op jit(solution)/shard_map/all_gather | solution.py:80
  559.6 127.3 %all-reduce.8.cloned.1.call-start = ((), (), s32[]{:S(2)}) async-start(), calls=%async_computation.18 | async-start | bytes 2097152 | tf_op jit(solution)/shard_map/psum | solution.py:84
  611.0 160.9 %reduce-scatter.19.cloned.1.call-start = ((), (), s32[]{:S(2)}) async-start(), calls=%async_computation.19 | async-start | bytes 278528 | tf_op jit(solution)/shard_map/reduce_scatter | solution.py:64
  688.5 5.6 copy-start.12
  688.6 2.9 collective-permute-start.1
  695.3 158.5 %reduce-scatter.21.cloned.1.call-start = ((), (), s32[]{:S(2)}) async-start(), calls=%async_computation.20 | async-start | bytes 1114112 | tf_op jit(solution)/shard_map/reduce_scatter | solution.py:61
  698.8 204.3 %all-gather.10.cloned.1.call-start = ((), (), s32[]{:S(2)}) async-start(), calls=%async_computation.21 | async-start | bytes 1114112 | tf_op jit(solution)/shard_map/all_gather | solution.py:80
  855.8 127.4 %all-reduce.10.cloned.1.call-start = ((), (), s32[]{:S(2)}) async-start(), calls=%async_computation.22 | async-start | bytes 2097152 | tf_op jit(solution)/shard_map/psum | solution.py:84
  907.3 162.1 %reduce-scatter.23.cloned.1.call-start = ((), (), s32[]{:S(2)}) async-start(), calls=%async_computation.23 | async-start | bytes 278528 | tf_op jit(solution)/shard_map/reduce_scatter | solution.py:64
  985.2 6.4 copy-start.13
  985.2 2.7 collective-permute-start.2
  992.8 158.4 %reduce-scatter.25.cloned.1.call-start = ((), (), s32[]{:S(2)}) async-start(), calls=%async_computation.24 | async-start | bytes 1114112 | tf_op jit(solution)/shard_map/reduce_scatter | solution.py:61
  996.3 204.0 %all-gather.12.cloned.1.call-start = ((), (), s32[]{:S(2)}) async-start(), calls=%async_computation.25 | async-start | bytes 1114112 | tf_op jit(solution)/shard_map/all_gather | solution.py:80
  1153.2 127.2 %all-reduce.12.cloned.1.call-start = ((), (), s32[]{:S(2)}) async-start(), calls=%async_computation.26 | async-start | bytes 2097152 | tf_op jit(solution)/shard_map/psum | solution.py:84
  1204.5 160.4 %reduce-scatter.27.cloned.1.call-start = ((), (), s32[]{:S(2)}) async-start(), calls=%async_computation.27 | async-start | bytes 278528 | tf_op jit(solution)/shard_map/reduce_scatter | solution.py:64
  1280.4 6.7 copy-start.14
  1283.4 2.7 collective-permute-start.3
  1288.2 158.4 %reduce-scatter.29.cloned.1.call-start = ((), (), s32[]{:S(2)}) async-start(), calls=%async_computation.28 | async-start | bytes 1114112 | tf_op jit(solution)/shard_map/reduce_scatter | solution.py:61
  1290.6 205.4 %all-gather.14.cloned.1.call-start = ((), (), s32[]{:S(2)}) async-start(), calls=%async_computation.29 | async-start | bytes 1114112 | tf_op jit(solution)/shard_map/all_gather | solution.py:80
  1448.7 127.4 %all-reduce.14.cloned.1.call-start = ((), (), s32[]{:S(2)}) async-start(), calls=%async_computation.30 | async-start | bytes 2097152 | tf_op jit(solution)/shard_map/psum | solution.py:84
  (9 other events, 14.9 us)
Sparse Core Ops, SparseCore 0:
  97.8 82.3 reduce-scatter.10
  183.7 78.5 reduce-scatter.12
  264.7 46.8 all-gather.5
  315.8 75.7 all-reduce.5
  399.3 76.4 reduce-scatter.14
  479.2 78.2 reduce-scatter.16
  560.0 46.8 all-gather.7
  611.1 75.7 all-reduce.7
  695.4 76.4 reduce-scatter.18
  775.3 78.4 reduce-scatter.20
  856.2 46.8 all-gather.9
  907.4 75.7 all-reduce.9
  992.9 76.4 reduce-scatter.22
  1072.7 78.3 reduce-scatter.24
  1153.4 46.8 all-gather.11
  1204.6 75.7 all-reduce.11
  1288.4 76.4 reduce-scatter.26
  1368.2 78.4 reduce-scatter.28
  1449.1 46.8 all-gather.13
  1500.3 75.7 all-reduce.13
where the time goes:
time: 1590 us
  waiting for transfers between devices  1270 us (80%)
  blocking collectives  185 us (12%)
  matrix products  48.2 us (3%)
  local copies, waits for them, and re-layouts  29.8 us (2%)
  other arithmetic  26 us (2%)
    reduce_scatter x5, waiting for transfers between devices, section_layer(): lax.psum_scatter(query_terms.astype(jnp.bfloat16), 'dp', scatter_dimensio...  405 us
    psum x5, waiting for transfers between devices, section_layer(): lax.psum(head_terms.astype(jnp.bfloat16), 'tensor').astype(jnp.float32)  379 us
    all_gather x5, waiting for transfers between devices, section_layer(): lax.all_gather(attended_rows, 'dp', axis=0, tiled=True)  236 us
    psum x5, blocking collectives, section_layer(): all_squares = lax.psum(square_terms, 'dp')  185 us
    reduce_scatter x5, waiting for transfers between devices, section_layer(): lax.psum_scatter(keyval_terms.astype(jnp.bfloat16), 'dp', scatter_dimensi...  185 us
    all_to_all x1, waiting for transfers between devices, on_device(): lax.all_to_all(tokens, 'dp', split_axis=1, concat_axis=0, tiled=True)  59.1 us
  transfers between devices with their start and end apart: 25, of which 25 were waited for; matrix products, arithmetic and copies ran while one was open for 1% of the time, Pallas kernels for 0%

commit v1 on v0

--- a/solution.py
+++ b/solution.py
@@ -77,7 +77,9 @@
         query_rows, key_value_rows, sentence_segment_rows, QUERY_HEADS // KEYVALUE_HEADS
     )
     head_terms = jnp.dot(
-        lax.all_gather(attended_rows, "dp", axis=0, tiled=True),
+        jnp.concatenate(
+            lax.all_to_all(jnp.stack([attended_rows] * lax.axis_size("dp")), "dp", 0, 0), axis=0
+        ),
         out_weight,
         preferred_element_type=jnp.float32,
     )

time: 1590 us -> 1430 us (0.90)
  waiting for transfers between devices: 1270 us -> 1030 us
  blocking collectives: 185 us -> 283 us
    all_gather x5 -> x0, waiting for transfers between devices: 236 us -> none  [section_layer(): lax.all_gather(attended_rows, 'dp', axis=0, tiled=True)]
    all_to_all x0 -> x5, blocking collectives: none -> 97.8 us  [section_layer(): lax.all_to_all(jnp.stack([attended_rows] * lax.axis_size('dp')), 'dp', 0, 0)]
  transfers between devices with their start and end apart: 25 -> 20, of which waited for: 25 -> 20; matrix products, arithmetic and copies ran while one was open for 1% -> 2% of each run, Pallas kernels for 0% -> 0%
where the time goes in v1:
time: 1430 us
  waiting for transfers between devices  1030 us (72%)
  blocking collectives  283 us (20%)
  matrix products  38.7 us (3%)
  local copies, waits for them, and re-layouts  27.3 us (2%)
  other arithmetic  26 us (2%)
    reduce_scatter x5, waiting for transfers between devices, section_layer(): lax.psum_scatter(query_terms.astype(jnp.bfloat16), 'dp', scatter_dimensio...  405 us
    psum x5, waiting for transfers between devices, section_layer(): lax.psum(head_terms.astype(jnp.bfloat16), 'tensor').astype(jnp.float32)  373 us
    psum x5, blocking collectives, section_layer(): all_squares = lax.psum(square_terms, 'dp')  185 us
    reduce_scatter x5, waiting for transfers between devices, section_layer(): lax.psum_scatter(keyval_terms.astype(jnp.bfloat16), 'dp', scatter_dimensi...  185 us
    all_to_all x5, blocking collectives, section_layer(): lax.all_to_all(jnp.stack([attended_rows] * lax.axis_size('dp')), 'dp', 0, 0)  97.8 us
    all_to_all x1, waiting for transfers between devices, on_device(): lax.all_to_all(tokens, 'dp', split_axis=1, concat_axis=0, tiled=True)  59.1 us
  transfers between devices with their start and end apart: 20, of which 20 were waited for; matrix products, arithmetic and copies ran while one was open for 2% of the time, Pallas kernels for 0%

profile of v1, /device:TPU:2, one launch (start us, length us, event | category | flops | bytes accessed | tf_op | source)
XLA Modules:
  0.0 1430.6 jit_solution(15268801265714493362)
XLA Ops:
  6.5 4.9 copy.87
  11.5 7.6 all-to-all-start
  19.2 59.1 %all-to-all-done = bf16[128,16,1024]{2,0,1:T(8,128)(2,1)} async-done(((bf16[128,16,1024]{2,0,1:T(8,128)(2,1)}), bf16[128,16,1024]{2,0,1:T(8,128)(2,1)}, u32[]{:S(2)}, u32[]{:S(2)}) %all-to-all-start) | async-done | bytes 4194336 | tf_op jit(solution)/shard_map/all_to_all | solution.py:91
  78.3 13.7 gather_fusion
  97.7 3.5 fusion.35
  103.8 39.7 %psum.70 = f32[512]{0:T(512)S(1)} all-reduce(f32[512]{0:T(512)S(1)} %fusion.1), channel_id=1, replica_groups=mesh['dp'=16,'section'=2,'tensor'=8] {'dp'}, use_global_device_ids=true, to_apply=%region_2.3 | all-reduce | flops 512 | bytes 4096 | tf_op jit(solution)/shard_map/psum | solution.py:58
  143.6 36.5 %reduce-scatter.11.cloned.1.call-done = bf16[32,256]{1,0:T(8,128)(2,1)} async-done(((bf16[512,256]{1,0:T(8,128)(2,1)}), bf16[32,256]{1,0:T(8,128)(2,1)}) %reduce-scatter.11.cloned.1.call-update) | async-done | bytes 16400 | tf_op jit(solution)/shard_map/reduce_scatter | solution.py:64
  180.9 81.1 %reduce-scatter.13.cloned.1.call-done = bf16[32,1024]{1,0:T(8,128)(2,1)} async-done(((bf16[512,1024]{1,0:T(8,128)(2,1)}), bf16[32,1024]{1,0:T(8,128)(2,1)}) %reduce-scatter.13.cloned.1.call-update) | async-done | bytes 65552 | tf_op jit(solution)/shard_map/reduce_scatter | solution.py:61
  263.6 19.6 %all_to_all.44 = bf16[16,32,1024]{2,1,0:T(8,128)(2,1)S(1)} all-to-all(bf16[16,32,1024]{2,1,0:T(8,128)(2,1)S(1)} %stack.15), channel_id=1, replica_groups=mesh['dp'=16,'section'=2,'tensor'=8] {'dp'}, dimensions={0} | all-to-all | bytes 2097152 | tf_op jit(solution)/shard_map/all_to_all | solution.py:81
  285.5 74.5 %all-reduce.6.cloned.1.call-done = bf16[512,1024]{1,0:T(8,128)(2,1)} async-done(((bf16[512,1024]{1,0:T(8,128)(2,1)}), bf16[512,1024]{1,0:T(8,128)(2,1)}) %all-reduce.6.cloned.1.call-update) | async-done | bytes 1048592 | tf_op jit(solution)/shard_map/psum | solution.py:86
  370.0 36.4 %psum.72 = f32[512]{0:T(512)S(1)} all-reduce(f32[512]{0:T(512)S(1)} %get-tuple-element.9), channel_id=1, replica_groups=mesh['dp'=16,'section'=2,'tensor'=8] {'dp'}, use_global_device_ids=true, to_apply=%region_8.9 | all-reduce | flops 512 | bytes 4096 | tf_op jit(solution)/shard_map/psum | solution.py:58
  406.5 37.8 %reduce-scatter.15.cloned.1.call-done = bf16[32,256]{1,0:T(8,128)(2,1)} async-done(((bf16[512,256]{1,0:T(8,128)(2,1)}), bf16[32,256]{1,0:T(8,128)(2,1)}) %reduce-scatter.15.cloned.1.call-update) | async-done | bytes 16400 | tf_op jit(solution)/shard_map/reduce_scatter | solution.py:64
  445.0 81.0 %reduce-scatter.17.cloned.1.call-done = bf16[32,1024]{1,0:T(8,128)(2,1)} async-done(((bf16[512,1024]{1,0:T(8,128)(2,1)}), bf16[32,1024]{1,0:T(8,128)(2,1)}) %reduce-scatter.17.cloned.1.call-update) | async-done | bytes 65552 | tf_op jit(solution)/shard_map/reduce_scatter | solution.py:61
  527.6 19.6 %all_to_all.45 = bf16[16,32,1024]{2,1,0:T(8,128)(2,1)S(1)} all-to-all(bf16[16,32,1024]{2,1,0:T(8,128)(2,1)S(1)} %stack.16), channel_id=1, replica_groups=mesh['dp'=16,'section'=2,'tensor'=8] {'dp'}, dimensions={0} | all-to-all | bytes 2097152 | tf_op jit(solution)/shard_map/all_to_all | solution.py:81
  549.4 74.6 %all-reduce.8.cloned.1.call-done = bf16[512,1024]{1,0:T(8,128)(2,1)} async-done(((bf16[512,1024]{1,0:T(8,128)(2,1)}), bf16[512,1024]{1,0:T(8,128)(2,1)}) %all-reduce.8.cloned.1.call-update) | async-done | bytes 1048592 | tf_op jit(solution)/shard_map/psum | solution.py:86
  632.5 3.5 fusion.41
  636.1 36.4 %psum.74 = f32[512]{0:T(512)S(1)} all-reduce(f32[512]{0:T(512)S(1)} %get-tuple-element.7), channel_id=1, replica_groups=mesh['dp'=16,'section'=2,'tensor'=8] {'dp'}, use_global_device_ids=true, to_apply=%region_14.15 | all-reduce | flops 512 | bytes 4096 | tf_op jit(solution)/shard_map/psum | solution.py:58
  672.6 36.5 %reduce-scatter.19.cloned.1.call-done = bf16[32,256]{1,0:T(8,128)(2,1)} async-done(((bf16[512,256]{1,0:T(8,128)(2,1)}), bf16[32,256]{1,0:T(8,128)(2,1)}) %reduce-scatter.19.cloned.1.call-update) | async-done | bytes 16400 | tf_op jit(solution)/shard_map/reduce_scatter | solution.py:64
  709.9 81.2 %reduce-scatter.21.cloned.1.call-done = bf16[32,1024]{1,0:T(8,128)(2,1)} async-done(((bf16[512,1024]{1,0:T(8,128)(2,1)}), bf16[32,1024]{1,0:T(8,128)(2,1)}) %reduce-scatter.21.cloned.1.call-update) | async-done | bytes 65552 | tf_op jit(solution)/shard_map/reduce_scatter | solution.py:61
  792.6 19.6 %all_to_all.46 = bf16[16,32,1024]{2,1,0:T(8,128)(2,1)S(1)} all-to-all(bf16[16,32,1024]{2,1,0:T(8,128)(2,1)S(1)} %stack.17), channel_id=1, replica_groups=mesh['dp'=16,'section'=2,'tensor'=8] {'dp'}, dimensions={0} | all-to-all | bytes 2097152 | tf_op jit(solution)/shard_map/all_to_all | solution.py:81
  814.5 74.6 %all-reduce.10.cloned.1.call-done = bf16[512,1024]{1,0:T(8,128)(2,1)} async-done(((bf16[512,1024]{1,0:T(8,128)(2,1)}), bf16[512,1024]{1,0:T(8,128)(2,1)}) %all-reduce.10.cloned.1.call-update) | async-done | bytes 1048592 | tf_op jit(solution)/shard_map/psum | solution.py:86
  898.8 3.5 fusion.44
  902.4 36.4 %psum.76 = f32[512]{0:T(512)S(1)} all-reduce(f32[512]{0:T(512)S(1)} %get-tuple-element.5), channel_id=1, replica_groups=mesh['dp'=16,'section'=2,'tensor'=8] {'dp'}, use_global_device_ids=true, to_apply=%region_20.21 | all-reduce | flops 512 | bytes 4096 | tf_op jit(solution)/shard_map/psum | solution.py:58
  938.9 36.5 %reduce-scatter.23.cloned.1.call-done = bf16[32,256]{1,0:T(8,128)(2,1)} async-done(((bf16[512,256]{1,0:T(8,128)(2,1)}), bf16[32,256]{1,0:T(8,128)(2,1)}) %reduce-scatter.23.cloned.1.call-update) | async-done | bytes 16400 | tf_op jit(solution)/shard_map/reduce_scatter | solution.py:64
  976.2 81.2 %reduce-scatter.25.cloned.1.call-done = bf16[32,1024]{1,0:T(8,128)(2,1)} async-done(((bf16[512,1024]{1,0:T(8,128)(2,1)}), bf16[32,1024]{1,0:T(8,128)(2,1)}) %reduce-scatter.25.cloned.1.call-update) | async-done | bytes 65552 | tf_op jit(solution)/shard_map/reduce_scatter | solution.py:61
  1058.9 19.6 %all_to_all.47 = bf16[16,32,1024]{2,1,0:T(8,128)(2,1)S(1)} all-to-all(bf16[16,32,1024]{2,1,0:T(8,128)(2,1)S(1)} %stack.18), channel_id=1, replica_groups=mesh['dp'=16,'section'=2,'tensor'=8] {'dp'}, dimensions={0} | all-to-all | bytes 2097152 | tf_op jit(solution)/shard_map/all_to_all | solution.py:81
  1080.8 74.6 %all-reduce.12.cloned.1.call-done = bf16[512,1024]{1,0:T(8,128)(2,1)} async-done(((bf16[512,1024]{1,0:T(8,128)(2,1)}), bf16[512,1024]{1,0:T(8,128)(2,1)}) %all-reduce.12.cloned.1.call-update) | async-done | bytes 1048592 | tf_op jit(solution)/shard_map/psum | solution.py:86
  1166.0 36.4 %psum.78 = f32[512]{0:T(512)S(1)} all-reduce(f32[512]{0:T(512)S(1)} %fusion.13), channel_id=1, replica_groups=mesh['dp'=16,'section'=2,'tensor'=8] {'dp'}, use_global_device_ids=true, to_apply=%region_26.27 | all-reduce | flops 512 | bytes 4096 | tf_op jit(solution)/shard_map/psum | solution.py:58
  1202.5 37.4 %reduce-scatter.27.cloned.1.call-done = bf16[32,256]{1,0:T(8,128)(2,1)} async-done(((bf16[512,256]{1,0:T(8,128)(2,1)}), bf16[32,256]{1,0:T(8,128)(2,1)}) %reduce-scatter.27.cloned.1.call-update) | async-done | bytes 16400 | tf_op jit(solution)/shard_map/reduce_scatter | solution.py:64
  1240.7 80.9 %reduce-scatter.29.cloned.1.call-done = bf16[32,1024]{1,0:T(8,128)(2,1)} async-done(((bf16[512,1024]{1,0:T(8,128)(2,1)}), bf16[32,1024]{1,0:T(8,128)(2,1)}) %reduce-scatter.29.cloned.1.call-update) | async-done | bytes 65552 | tf_op jit(solution)/shard_map/reduce_scatter | solution.py:61
  1323.2 19.6 %all_to_all.48 = bf16[16,32,1024]{2,1,0:T(8,128)(2,1)S(1)} all-to-all(bf16[16,32,1024]{2,1,0:T(8,128)(2,1)S(1)} %stack.19), channel_id=1, replica_groups=mesh['dp'=16,'section'=2,'tensor'=8] {'dp'}, dimensions={0} | all-to-all | bytes 2097152 | tf_op jit(solution)/shard_map/all_to_all | solution.py:81
  1345.1 74.6 %all-reduce.14.cloned.1.call-done = bf16[512,1024]{1,0:T(8,128)(2,1)} async-done(((bf16[512,1024]{1,0:T(8,128)(2,1)}), bf16[512,1024]{1,0:T(8,128)(2,1)}) %all-reduce.14.cloned.1.call-update) | async-done | bytes 1048592 | tf_op jit(solution)/shard_map/psum | solution.py:86
  (147 shorter events, 74.8 us)
Async XLA Ops:
  6.5 91.2 %copy-start = (bf16[1,1024,1024]{2,1,0:T(8,128)(2,1)S(1)}, bf16[1,1024,1024]{2,1,0:T(8,128)(2,1)}, u32[]{:S(2)}) copy-start(bf16[1,1024,1024]{2,1,0:T(8,128)(2,1)} %param.11) | copy-start | bytes 6291460
  11.5 7.7 copy-start.9
  11.5 66.8 %all-to-all-start = ((bf16[128,16,1024]{2,0,1:T(8,128)(2,1)}), bf16[128,16,1024]{2,0,1:T(8,128)(2,1)}, u32[]{:S(2)}, u32[]{:S(2)}) async-start(bf16[128,16,1024]{2,0,1:T(8,128)(2,1)} %bitcast.271), calls=%async_computation | async-start | bytes 8388608 | tf_op jit(solution)/shard_map/all_to_all | solution.py:91
  19.1 161.0 %reduce-scatter.11.cloned.1.call-start = ((), (), s32[]{:S(2)}) async-start(), calls=%async_computation.16 | async-start | bytes 278528 | tf_op jit(solution)/shard_map/reduce_scatter | solution.py:64
  92.0 4.5 copy-start.15
  92.0 4.5 copy-start.20
  97.7 164.4 %reduce-scatter.13.cloned.1.call-start = ((), (), s32[]{:S(2)}) async-start(), calls=%async_computation.17 | async-start | bytes 1114112 | tf_op jit(solution)/shard_map/reduce_scatter | solution.py:61
  101.2 258.8 %all-reduce.6.cloned.1.call-start = ((), (), s32[]{:S(2)}) async-start(), calls=%async_computation.18 | async-start | bytes 2097152 | tf_op jit(solution)/shard_map/psum | solution.py:86
  263.2 20.0 %copy-start.10 = (bf16[1,1024,1024]{2,1,0:T(8,128)(2,1)S(1)}, bf16[1,1024,1024]{2,1,0:T(8,128)(2,1)}, u32[]{:S(2)}) copy-start(bf16[1,1024,1024]{2,1,0:T(8,128)(2,1)} %param.13) | copy-start | bytes 6291460
  285.4 158.8 %reduce-scatter.15.cloned.1.call-start = ((), (), s32[]{:S(2)}) async-start(), calls=%async_computation.19 | async-start | bytes 278528 | tf_op jit(solution)/shard_map/reduce_scatter | solution.py:64
  362.0 2.7 collective-permute-start
  367.6 158.4 %reduce-scatter.17.cloned.1.call-start = ((), (), s32[]{:S(2)}) async-start(), calls=%async_computation.20 | async-start | bytes 1114112 | tf_op jit(solution)/shard_map/reduce_scatter | solution.py:61
  369.9 254.2 %all-reduce.8.cloned.1.call-start = ((), (), s32[]{:S(2)}) async-start(), calls=%async_computation.21 | async-start | bytes 2097152 | tf_op jit(solution)/shard_map/psum | solution.py:86
  527.2 20.0 %copy-start.11 = (bf16[1,1024,1024]{2,1,0:T(8,128)(2,1)S(1)}, bf16[1,1024,1024]{2,1,0:T(8,128)(2,1)}, u32[]{:S(2)}) copy-start(bf16[1,1024,1024]{2,1,0:T(8,128)(2,1)} %param.13) | copy-start | bytes 6291460
  549.4 159.7 %reduce-scatter.19.cloned.1.call-start = ((), (), s32[]{:S(2)}) async-start(), calls=%async_computation.22 | async-start | bytes 278528 | tf_op jit(solution)/shard_map/reduce_scatter | solution.py:64
  625.7 5.6 copy-start.17
  625.7 2.9 collective-permute-start.1
  632.5 158.6 %reduce-scatter.21.cloned.1.call-start = ((), (), s32[]{:S(2)}) async-start(), calls=%async_computation.23 | async-start | bytes 1114112 | tf_op jit(solution)/shard_map/reduce_scatter | solution.py:61
  636.0 253.2 %all-reduce.10.cloned.1.call-start = ((), (), s32[]{:S(2)}) async-start(), calls=%async_computation.24 | async-start | bytes 2097152 | tf_op jit(solution)/shard_map/psum | solution.py:86
  792.2 20.0 %copy-start.12 = (bf16[1,1024,1024]{2,1,0:T(8,128)(2,1)S(1)}, bf16[1,1024,1024]{2,1,0:T(8,128)(2,1)}, u32[]{:S(2)}) copy-start(bf16[1,1024,1024]{2,1,0:T(8,128)(2,1)} %param.13) | copy-start | bytes 6291460
  814.5 160.9 %reduce-scatter.23.cloned.1.call-start = ((), (), s32[]{:S(2)}) async-start(), calls=%async_computation.25 | async-start | bytes 278528 | tf_op jit(solution)/shard_map/reduce_scatter | solution.py:64
  891.1 6.4 copy-start.18
  891.1 2.7 collective-permute-start.2
  898.7 158.6 %reduce-scatter.25.cloned.1.call-start = ((), (), s32[]{:S(2)}) async-start(), calls=%async_computation.26 | async-start | bytes 1114112 | tf_op jit(solution)/shard_map/reduce_scatter | solution.py:61
  902.3 253.1 %all-reduce.12.cloned.1.call-start = ((), (), s32[]{:S(2)}) async-start(), calls=%async_computation.27 | async-start | bytes 2097152 | tf_op jit(solution)/shard_map/psum | solution.py:86
  1058.5 20.0 %copy-start.13 = (bf16[1,1024,1024]{2,1,0:T(8,128)(2,1)S(1)}, bf16[1,1024,1024]{2,1,0:T(8,128)(2,1)}, u32[]{:S(2)}) copy-start(bf16[1,1024,1024]{2,1,0:T(8,128)(2,1)} %param.13) | copy-start | bytes 6291460
  1080.7 159.2 %reduce-scatter.27.cloned.1.call-start = ((), (), s32[]{:S(2)}) async-start(), calls=%async_computation.28 | async-start | bytes 278528 | tf_op jit(solution)/shard_map/reduce_scatter | solution.py:64
  1155.4 6.7 copy-start.19
  1158.4 2.7 collective-permute-start.3
  1163.2 158.4 %reduce-scatter.29.cloned.1.call-start = ((), (), s32[]{:S(2)}) async-start(), calls=%async_computation.29 | async-start | bytes 1114112 | tf_op jit(solution)/shard_map/reduce_scatter | solution.py:61
  1165.6 254.2 %all-reduce.14.cloned.1.call-start = ((), (), s32[]{:S(2)}) async-start(), calls=%async_computation.30 | async-start | bytes 2097152 | tf_op jit(solution)/shard_map/psum | solution.py:86
  1322.8 20.0 %copy-start.14 = (bf16[1,1024,1024]{2,1,0:T(8,128)(2,1)S(1)}, bf16[1,1024,1024]{2,1,0:T(8,128)(2,1)}, u32[]{:S(2)}) copy-start(bf16[1,1024,1024]{2,1,0:T(8,128)(2,1)} %param.13) | copy-start | bytes 6291460
  (9 other events, 15.0 us)
Sparse Core Ops, SparseCore 0:
  97.8 82.2 reduce-scatter.10
  183.6 78.3 reduce-scatter.12
  285.5 74.4 all-reduce.5
  367.7 76.4 reduce-scatter.14
  447.6 78.3 reduce-scatter.16
  549.5 74.4 all-reduce.7
  632.6 76.4 reduce-scatter.18
  712.6 78.4 reduce-scatter.20
  814.6 74.5 all-reduce.9
  898.8 76.4 reduce-scatter.22
  978.9 78.4 reduce-scatter.24
  1080.9 74.4 all-reduce.11
  1163.4 76.5 reduce-scatter.26
  1243.3 78.3 reduce-scatter.28
  1345.2 74.4 all-reduce.13
